TPU v7x, 256 devices: a whole 4x4x8 slice. The times are simulated.
256 devices in a mesh: grp: 4 (over x), tok: 8 (over z), mdl: 8 (over y, core).
Axes of the slice: x: 4, y: 4, z: 8, core: 2. Of those that a mesh axis runs over, the one named last changes fastest.
Arguments:
- hidden_in: bfloat16 [4, 1024, 5120], P('grp', 'tok', 'mdl'), may hold values from -8 to 8
- seg_ids: int32 [4, 1024], replicated, may hold values from 0 to 3, never falling along the last dimension, each value on 1 to 768 neighbouring positions
- request_prefix: int32 [4, 4], replicated, may hold values from 0 to 1
- page_table: int32 [32], replicated, may hold values from 0 to 31, each once
- prefix_cache: bfloat16 [32, 256, 8, 256], P(('grp', 'mdl'), None, 'tok'), may hold values from -200 to 200
- attn_gain: float32 [5120], P('mdl'), may hold values from 0.1 to 1.9
- w_query: bfloat16 [5120, 5120], P('mdl', 'tok'), may hold values from -0.078125 to 0.078125
- w_key: bfloat16 [5120, 1024], P('mdl', 'tok'), may hold values from -0.25 to 0.25
- w_value: bfloat16 [5120, 1024], P('mdl', 'tok'), may hold values from -0.078125 to 0.078125
- w_out: bfloat16 [5120, 5120], P('tok', 'mdl'), may hold values from -0.078125 to 0.078125
- ffn_gain: float32 [5120], P('mdl'), may hold values from 0.1 to 1.9
- w_gate: bfloat16 [5120, 14336], P('mdl', 'tok'), may hold values from -0.078125 to 0.078125
- w_up: bfloat16 [5120, 14336], P('mdl', 'tok'), may hold values from -0.078125 to 0.078125
- w_down: bfloat16 [14336, 5120], P('tok', 'mdl'), may hold values from -0.046875 to 0.046875
- final_gain: float32 [5120], replicated, may hold values from 0.1 to 1.9
- lm_head: bfloat16 [76800, 5120], P(('grp', 'tok', 'mdl')), may hold values from -0.25 to 0.25
Outputs:
- hidden_out: bfloat16 [4, 1024, 5120], P('grp', 'tok', 'mdl')
- new_kv: bfloat16 [4, 1024, 8, 256], P('grp', 'mdl', 'tok')
- req_norm: float32 [4, 4], P('grp')
- max_logit: float32 [4, 4], replicated
- logits: float32 [16, 76800], P(None, ('grp', 'tok', 'mdl'))
Inputs may be any that keep to these rules, and one draw needn't show every extreme that they name: `seg_ids`: requests of a group are contiguous, in order, and none is empty. `page_table`: each physical slot holds exactly one logical page.
All inputs are finite; a program needn't handle non-finite values.
Results may differ from a plain program's by a relative error of at most 0.024.
Values may be sent and summed in bfloat16 or wider, within the bound.
No kernel may reach another device: no remote copies, remote signals or barrier semaphores. Data moves between devices by JAX's collectives and lax.ppermute only.
A program may use at most 128 MiB of HBM per device.

v0:
```python
import jax
import jax.numpy as jnp
from jax import lax
from jax.sharding import PartitionSpec as P

PREFIX = 4096
PAGE = 256
EPS = 1e-06
THETA = 1000000.0
NEG = -1e30


def rotate(tensor, positions):
    half_dim = tensor.shape[-1] // 2
    frequency = THETA ** (-(jnp.arange(half_dim, dtype=jnp.float32) * 2.0 / tensor.shape[-1]))
    angles = positions.astype(jnp.float32)[:, None] * frequency[None, :]
    cosine = jnp.cos(angles)[:, None, :]
    sine_part = jnp.sin(angles)[:, None, :]
    first_part = tensor[..., :half_dim]
    second = tensor[..., half_dim:]
    return jnp.concatenate(
        [first_part * cosine - second * sine_part, second * cosine + first_part * sine_part], -1
    )


def on_device(
    hidden_in,
    seg_ids,
    request_prefix,
    page_table,
    prefix_cache,
    attn_gain,
    w_query,
    w_key,
    w_value,
    w_out,
    ffn_gain,
    w_gate,
    w_up,
    w_down,
    final_gain,
    lm_head,
):
    groups_total = seg_ids.shape[0]
    seq_len = seg_ids.shape[1]
    req_count = request_prefix.shape[1]
    tok_rows = hidden_in.shape[1]
    feat_dev = hidden_in.shape[2]
    model_width = feat_dev * lax.axis_size("mdl")
    head_dim = prefix_cache.shape[3] // 2
    kv_dev = prefix_cache.shape[2]
    heads_dev = w_query.shape[1] // head_dim
    group_size = heads_dev // kv_dev
    page_len = prefix_cache.shape[1]
    slot_total = page_table.shape[0]
    rows_mdl = seq_len // lax.axis_size("mdl")
    group_idx = lax.axis_index("grp")
    tok_idx = lax.axis_index("tok")
    mdl_idx = lax.axis_index("mdl")
    score_scale = head_dim ** (-0.5)
    tokens = hidden_in[0].astype(jnp.float32)
    squares = lax.psum(jnp.sum(tokens * tokens, -1), "mdl")
    normed = (tokens * lax.rsqrt(squares[:, None] / model_width + EPS) * attn_gain).astype(
        jnp.bfloat16
    )
    w_joined = jnp.concatenate([w_query, w_key, w_value], 1)
    partial_qkv = jnp.dot(
        lax.all_gather(normed, "tok", axis=0, tiled=True),
        w_joined,
        preferred_element_type=jnp.float32,
    )
    qkv_rows = lax.psum_scatter(partial_qkv, "mdl", scatter_dimension=0, tiled=True)
    q_cols = heads_dev * head_dim
    kv_cols = kv_dev * head_dim
    queries = qkv_rows[:, :q_cols].reshape(rows_mdl, heads_dev, head_dim)
    key_rows = qkv_rows[:, q_cols : q_cols + kv_cols].reshape(rows_mdl, kv_dev, head_dim)
    value_rows = qkv_rows[:, q_cols + kv_cols :].reshape(rows_mdl, kv_dev, head_dim)
    seg_row = lax.dynamic_index_in_dim(seg_ids, group_idx, 0, keepdims=False)
    prefix_row = lax.dynamic_index_in_dim(request_prefix, group_idx, 0, keepdims=False)
    requests = jnp.arange(req_count, dtype=jnp.int32)
    member = seg_row[:, None] == requests[None, :]
    counts = jnp.sum(member.astype(jnp.int32), 0)
    offsets = jnp.cumsum(counts) - counts
    row_start = mdl_idx * rows_mdl
    my_rows = row_start + jnp.arange(rows_mdl, dtype=jnp.int32)
    my_seg = lax.dynamic_slice_in_dim(seg_row, row_start, rows_mdl)
    my_member = my_seg[:, None] == requests[None, :]
    positions = PREFIX + my_rows - jnp.sum(jnp.where(my_member, offsets[None, :], 0), 1)
    my_prefix = jnp.sum(jnp.where(my_member, prefix_row[None, :], 0), 1)
    q_rot = (
        rotate(queries, positions)
        .astype(jnp.bfloat16)
        .reshape(rows_mdl, kv_dev, group_size, head_dim)
    )
    k_rot = rotate(key_rows, positions).astype(jnp.bfloat16)
    appended = jnp.concatenate([k_rot, value_rows.astype(jnp.bfloat16)], -1)
    suffix = lax.all_gather(appended, "mdl", axis=0, tiled=True)
    every_row = jnp.arange(seq_len, dtype=jnp.int32)
    suffix_ok = ((seg_row[None, :] == my_seg[:, None]) & (every_row[None, :] <= my_rows[:, None]))[
        :, None, None, :
    ]
    suffix_scores = (
        jnp.einsum(
            "rcgd,tcd->rcgt", q_rot, suffix[..., :head_dim], preferred_element_type=jnp.float32
        )
        * score_scale
    )
    suffix_scores = jnp.where(suffix_ok, suffix_scores, NEG)
    row_max = jnp.max(suffix_scores, -1)
    suffix_weights = jnp.where(suffix_ok, jnp.exp(suffix_scores - row_max[..., None]), 0.0)
    row_total = jnp.sum(suffix_weights, -1)
    mixed = jnp.einsum(
        "rcgt,tcd->rcgd",
        suffix_weights.astype(jnp.bfloat16),
        suffix[..., head_dim:],
        preferred_element_type=jnp.float32,
    )
    slot_ids = jnp.arange(slot_total, dtype=jnp.int32)
    pages_each = PREFIX // PAGE
    slot_prefix = jnp.sum(
        jnp.where(page_table[None, :] == slot_ids[:, None], (slot_ids // pages_each)[None, :], 0), 1
    )
    piece = lax.all_gather(prefix_cache, ("grp", "mdl"), axis=0, tiled=True)
    page_count = piece.shape[0]
    key_prefix = jnp.repeat(slot_prefix, page_len)
    allowed = (my_prefix[:, None] == key_prefix[None, :])[:, None, None, :]
    flat_pages = piece.reshape(page_count * page_len, kv_dev, 2 * head_dim)
    scores = (
        jnp.einsum(
            "rcgd,kcd->rcgk", q_rot, flat_pages[..., :head_dim], preferred_element_type=jnp.float32
        )
        * score_scale
    )
    scores = jnp.where(allowed, scores, NEG)
    new_max = jnp.maximum(row_max, jnp.max(scores, -1))
    factor = jnp.exp(row_max - new_max)
    page_weights = jnp.where(allowed, jnp.exp(scores - new_max[..., None]), 0.0)
    new_total = row_total * factor + jnp.sum(page_weights, -1)
    new_mixed = mixed * factor[..., None] + jnp.einsum(
        "rcgk,kcd->rcgd",
        page_weights.astype(jnp.bfloat16),
        flat_pages[..., head_dim:],
        preferred_element_type=jnp.float32,
    )
    attended = (
        (new_mixed / new_total[..., None])
        .astype(jnp.bfloat16)
        .reshape(rows_mdl, heads_dev * head_dim)
    )
    partial_out = jnp.dot(
        lax.all_gather(attended, "mdl", axis=0, tiled=True),
        w_out,
        preferred_element_type=jnp.float32,
    )
    residual = tokens + lax.psum_scatter(
        partial_out.astype(jnp.bfloat16), "tok", scatter_dimension=0, tiled=True
    ).astype(jnp.float32)
    squares_ffn = lax.psum(jnp.sum(residual * residual, -1), "mdl")
    ffn_input = (residual * lax.rsqrt(squares_ffn[:, None] / model_width + EPS) * ffn_gain).astype(
        jnp.bfloat16
    )
    w_pair = jnp.concatenate([w_gate, w_up], 1)
    ff_dev = w_gate.shape[1]
    partial_ffn = jnp.dot(
        lax.all_gather(ffn_input, "tok", axis=0, tiled=True),
        w_pair,
        preferred_element_type=jnp.float32,
    )
    summed = lax.psum_scatter(
        partial_ffn.astype(jnp.bfloat16), "mdl", scatter_dimension=0, tiled=True
    ).astype(jnp.float32)
    activated = (jax.nn.silu(summed[:, :ff_dev]) * summed[:, ff_dev:]).astype(jnp.bfloat16)
    partial_down = jnp.dot(
        lax.all_gather(activated, "mdl", axis=0, tiled=True),
        w_down,
        preferred_element_type=jnp.float32,
    )
    final_rows = residual + lax.psum_scatter(
        partial_down.astype(jnp.bfloat16), "tok", scatter_dimension=0, tiled=True
    ).astype(jnp.float32)
    tok_start = tok_idx * tok_rows
    my_tok_rows = tok_start + jnp.arange(tok_rows, dtype=jnp.int32)
    tok_seg = lax.dynamic_slice_in_dim(seg_row, tok_start, tok_rows)
    row_squares = jnp.sum(final_rows * final_rows, -1)
    req_squares = jnp.sum(
        jnp.where(tok_seg[:, None] == requests[None, :], row_squares[:, None], 0.0), 0
    )
    ends = offsets + counts - 1
    picked = ends[:, None] == my_tok_rows[None, :]
    last_part = jnp.sum(jnp.where(picked[:, :, None], final_rows[None, :, :], 0.0), 1)
    padded = jnp.zeros((groups_total * req_count, model_width), jnp.float32)
    padded = lax.dynamic_update_slice(
        padded, last_part, (group_idx * req_count, mdl_idx * feat_dev)
    )
    req_total = lax.psum(req_squares, ("tok", "mdl"))
    last_all = lax.psum(padded, ("grp", "tok", "mdl"))
    req_norm = jnp.sqrt(req_total / (counts.astype(jnp.float32) * model_width) + EPS)
    last_normed = (
        last_all * lax.rsqrt(jnp.mean(last_all * last_all, -1, keepdims=True) + EPS) * final_gain
    ).astype(jnp.bfloat16)
    logits = lax.dot_general(
        last_normed, lm_head, (((1,), (1,)), ((), ())), preferred_element_type=jnp.float32
    )
    max_logit = lax.pmax(jnp.max(logits, -1), ("grp", "tok", "mdl")).reshape(
        groups_total, req_count
    )
    return (
        final_rows.astype(jnp.bfloat16)[None],
        appended[None],
        req_norm[None],
        max_logit,
        logits,
    )


def solution(mesh):
    return jax.shard_map(
        on_device,
        mesh=mesh,
        in_specs=(
            P("grp", "tok", "mdl"),
            P(),
            P(),
            P(),
            P(("grp", "mdl"), None, "tok", None),
            P("mdl"),
            P("mdl", "tok"),
            P("mdl", "tok"),
            P("mdl", "tok"),
            P("tok", "mdl"),
            P("mdl"),
            P("mdl", "tok"),
            P("mdl", "tok"),
            P("tok", "mdl"),
            P(),
            P(("grp", "tok", "mdl"), None),
        ),
        out_specs=(
            P("grp", "tok", "mdl"),
            P("grp", "mdl", "tok", None),
            P("grp", None),
            P(),
            P(None, ("grp", "tok", "mdl")),
        ),
        check_vma=False,
    )
```

profile of v0, /device:TPU:1, one launch (start us, length us, event | category | flops | bytes accessed | tf_op | source)
XLA Modules:
  0.0 899.1 jit_solution(10230812188905599163)
XLA Ops:
  8.1 1.2 fusion.44
  9.2 15.0 %psum.28 = f32[128]{0:T(128)S(1)} all-reduce(f32[128]{0:T(128)S(1)} %fusion.44), channel_id=1, replica_groups=mesh['grp'=4,'tok'=8,'mdl'=8] {'mdl'}, use_global_device_ids=true, to_apply=%region_1.0 | all-reduce | flops 128 | bytes 1024 | tf_op jit(solution)/shard_map/psum | solution.py:62
  24.2 1.7 fusion.46
  26.0 35.1 %all-gather.6.cloned.1.call-done = bf16[1024,640]{1,0:T(8,128)(2,1)} async-done(((bf16[128,640]{1,0:T(8,128)(2,1)}), bf16[1024,640]{1,0:T(8,128)(2,1)}) %all-gather.6.cloned.1.call-update) | async-done | bytes 1310736 | tf_op jit(solution)/shard_map/all_gather | solution.py:68
  61.1 5.1 fusion.30
  66.3 0.5 all-gather.8.cloned.1.call-update
  66.9 0.1 select_reduce_fusion.1
  67.0 0.1 broadcast_bitcast_fusion
  67.2 0.7 constant_dynamic-slice_fusion
  67.9 0.1 convert_reduce_fusion
  68.0 0.2 reduce-window.7
  68.2 0.7 dynamic-slice_bitcast_fusion.1
  68.9 0.8 dynamic-slice_bitcast_fusion
  69.7 0.1 select_reduce_fusion.3
  69.8 1.0 multiply_cosine_fusion
  70.8 0.8 fusion.43
  71.6 1.6 broadcast_compare_fusion
  73.3 34.7 %reduce-scatter.5.cloned.1.call-done = f32[128,896]{0,1:T(8,128)} async-done(((f32[1024,896]{0,1:T(8,128)}), f32[128,896]{0,1:T(8,128)}) %reduce-scatter.5.cloned.1.call-update) | async-done | bytes 458768 | tf_op jit(solution)/shard_map/reduce_scatter | solution.py:72
  107.9 1.0 slice.59
  108.9 0.7 fusion.71
  109.7 1.1 copy.58
  110.8 1.8 copy.57
  112.6 0.8 slice_bitcast_fusion.10
  113.5 0.2 fusion.56
  113.7 0.8 fusion.59
  114.5 16.8 %all_gather.19 = bf16[1024,1,256]{0,2,1:T(8,128)(2,1)} all-gather(bf16[128,1,256]{0,2,1:T(8,128)(2,1)S(1)} %get-tuple-element.23), channel_id=1, replica_groups=mesh['grp'=4,'tok'=8,'mdl'=8] {'mdl'}, dimensions={0}, use_global_device_ids=true | all-gather | bytes 589824 | tf_op jit(solution)/shard_map/all_gather | solution.py:97
  131.3 1.8 subtract_convert_fusion
  133.1 12.9 %fusion = (f32[128,5]{0,1:T(8,128)S(1)}, f32[128,5,8192]{2,0,1:T(8,128)}) fusion(pred[128,8192]{1,0:T(8,128)(4,1)} %broadcast_compare_fusion, bf16[8192,1,256]{2,0,1:T(8,128)(2,1)} %bitcast.150, bf16[128,5,64]{2,0,1:T(8,128)(2,1)} %get-tuple-element.17, bf16[128,5,64]{2,0,1:T(8,128)(2,1)} %get-tuple-element.16), kind=kOutput, calls=%fused_computation.2 | convolution fusion | flops 1358232960 | bytes 24447488 | tf_op jit(solution)/shard_map/rcgd,kcd->rcgk/dot_general | solution.py:129
  146.1 2.2 fusion.10
  148.3 14.2 %fusion.21 = f32[1,128,128,5]{2,1,3,0:T(8,128)} fusion(bf16[8192,1,256]{2,0,1:T(8,128)(2,1)} %bitcast.151, f32[128,5,8192]{2,0,1:T(8,128)} %get-tuple-element.33, f32[128,5]{0,1:T(8,128)S(1)} %max.19, pred[128,8192]{1,0:T(8,128)(4,1)} %broadcast_compare_fusion), kind=kOutput, calls=%fused_computation.28 | convolution fusion | flops 1368391680 | bytes 24447488 | tf_op jit(solution)/shard_map/rcgk,kcd->rcgd/dot_general | solution.py:139
  162.5 10.7 %fusion.1 = f32[128,5]{0,1:T(8,128)S(1)} fusion(f32[128,5,8192]{2,0,1:T(8,128)} %get-tuple-element.33, f32[128,5]{0,1:T(8,128)S(1)} %max.19, pred[128,8192]{1,0:T(8,128)(4,1)} %broadcast_compare_fusion), kind=kLoop, calls=%fused_computation.3 | loop fusion | flops 26213760 | bytes 22025216 | tf_op jit(solution)/shard_map/reduce_sum | solution.py:138
  173.2 0.6 fusion.12
  173.9 0.3 copy-done.6
  174.2 0.1 copy-done.13
  174.3 1.5 fusion.39
  175.9 27.0 %all-gather.10.cloned.1.call-done = bf16[1024,640]{0,1:T(8,128)(2,1)} async-done(((bf16[128,640]{0,1:T(8,128)(2,1)}), bf16[1024,640]{0,1:T(8,128)(2,1)}) %all-gather.10.cloned.1.call-update) | async-done | bytes 1310736 | tf_op jit(solution)/shard_map/all_gather | solution.py:151
  202.9 4.0 convolution_convert_fusion.2
  206.9 36.2 %reduce-scatter.7.cloned.1.call-done = bf16[128,640]{1,0:T(8,128)(2,1)} async-done(((bf16[1024,640]{1,0:T(8,128)(2,1)}), bf16[128,640]{1,0:T(8,128)(2,1)}) %reduce-scatter.7.cloned.1.call-update) | async-done | bytes 163856 | tf_op jit(solution)/shard_map/reduce_scatter | solution.py:155
  243.2 1.1 multiply_reduce_fusion.2
  244.2 16.7 %psum.29 = f32[128]{0:T(128)S(1)} all-reduce(f32[128]{0:T(128)S(1)} %multiply_reduce_fusion.2), channel_id=1, replica_groups=mesh['grp'=4,'tok'=8,'mdl'=8] {'mdl'}, use_global_device_ids=true, to_apply=%region_14.15 | all-reduce | flops 128 | bytes 1024 | tf_op jit(solution)/shard_map/psum | solution.py:158
  260.9 1.7 multiply_convert_fusion.1
  262.7 30.4 %all-gather.12.cloned.1.call-done = bf16[1024,640]{1,0:T(8,128)(2,1)} async-done(((bf16[128,640]{1,0:T(8,128)(2,1)}), bf16[1024,640]{1,0:T(8,128)(2,1)}) %all-gather.12.cloned.1.call-update) | async-done | bytes 1310736 | tf_op jit(solution)/shard_map/all_gather | solution.py:165
  293.1 10.5 %convolution_convert_fusion = bf16[1024,3584]{1,0:T(8,128)(2,1)} fusion(bf16[1024,640]{1,0:T(8,128)(2,1)} %all-gather.12.cloned.1.call-done, bf16[640,1792]{1,0:T(8,128)(2,1)} %param.28, bf16[640,1792]{1,0:T(8,128)(2,1)} %param.27), kind=kOutput, calls=%fused_computation.8 | convolution fusion | flops 4710465536 | bytes 13238272 | tf_op jit(solution)/shard_map/dot_general | solution.py:164
  303.6 53.3 %reduce-scatter.9.cloned.1.call-done = bf16[128,3584]{1,0:T(8,128)(2,1)} async-done(((bf16[1024,3584]{1,0:T(8,128)(2,1)}), bf16[128,3584]{1,0:T(8,128)(2,1)}) %reduce-scatter.9.cloned.1.call-update) | async-done | bytes 917520 | tf_op jit(solution)/shard_map/reduce_scatter | solution.py:169
  356.9 1.4 convert_element_type.96
  358.3 1.0 fusion.42
  359.4 33.1 %all-gather.14.cloned.1.call-done = bf16[1024,1792]{1,0:T(8,128)(2,1)} async-done(((bf16[128,1792]{1,0:T(8,128)(2,1)}), bf16[1024,1792]{1,0:T(8,128)(2,1)}) %all-gather.14.cloned.1.call-update) | async-done | bytes 3670032 | tf_op jit(solution)/shard_map/all_gather | solution.py:174
  392.5 6.8 convolution_convert_fusion.1
  399.4 0.1 broadcast_compare_fusion.1
  399.5 35.1 %reduce-scatter.11.cloned.1.call-done = bf16[128,640]{1,0:T(8,128)(2,1)} async-done(((bf16[1024,640]{1,0:T(8,128)(2,1)}), bf16[128,640]{1,0:T(8,128)(2,1)}) %reduce-scatter.11.cloned.1.call-update) | async-done | bytes 163856 | tf_op jit(solution)/shard_map/reduce_scatter | solution.py:178
  434.6 1.7 multiply_reduce_fusion.1
  436.3 0.1 select_reduce_fusion.2
  436.4 0.7 copy.50
  437.2 128.3 %psum.30 = f32[4]{0:T(128)S(1)} all-reduce(f32[4]{0:T(128)S(1)} %select_reduce_fusion.2), channel_id=1, replica_groups=mesh['grp'=4,'tok'=8,'mdl'=8] {'tok','mdl'}, use_global_device_ids=true, to_apply=%region_19.20 | all-reduce | flops 4 | bytes 32 | tf_op jit(solution)/shard_map/psum | solution.py:195
  565.5 1.2 select_reduce_fusion
  566.7 0.7 dynamic_update_slice.3
  567.5 0.7 copy-done.4
  568.2 1.7 convert_bitcast_fusion
  569.9 243.1 %all-reduce.2.cloned.1.call-done = f32[16,5120]{1,0:T(8,128)} async-done(((f32[16,5120]{1,0:T(8,128)}), f32[16,5120]{1,0:T(8,128)}) %all-reduce.2.cloned.1.call-update) | async-done | bytes 327696 | tf_op jit(solution)/shard_map/psum | solution.py:196
  813.0 1.1 multiply_reduce_fusion
  814.1 2.6 fusion.72
  816.8 0.1 reshape.445
  816.9 0.5 sqrt_bitcast_fusion
  817.4 74.3 %pmax.7 = f32[4,4]{1,0:T(4,128)} all-reduce(f32[4,4]{1,0:T(4,128)S(1)} %reshape.445), channel_id=1, replica_groups=mesh['grp'=4,'tok'=8,'mdl'=8] {'grp','tok','mdl'}, use_global_device_ids=true, to_apply=%region_24.25 | all-reduce | flops 16 | bytes 128 | tf_op jit(solution)/shard_map/pmax | solution.py:204
  (59 shorter events, 0.8 us)
Async XLA Ops:
  8.0 806.1 %copy-start = (bf16[300,5120]{1,0:T(8,128)(2,1)S(1)}, bf16[300,5120]{1,0:T(8,128)(2,1)}, u32[]{:S(2)}) copy-start(bf16[300,5120]{1,0:T(8,128)(2,1)} %param.31) | copy-start | bytes 9216004
  8.0 53.1 %all-gather.6.cloned.1.call-start = ((), (), s32[]{:S(2)}) async-start(), calls=%async_computation.4 | async-start | bytes 1474560 | tf_op jit(solution)/shard_map/all_gather | solution.py:68
  25.9 82.0 %reduce-scatter.5.cloned.1.call-start = ((), (), s32[]{:S(2)}) async-start(), calls=%async_computation.5 | async-start | bytes 4128768 | tf_op jit(solution)/shard_map/reduce_scatter | solution.py:72
  66.2 0.7 copy-start.12
  66.3 66.8 %all-gather.8.cloned.1.call-start = ((), (), s32[]{:S(2)}) async-start(), calls=%async_computation.6 | async-start | bytes 4325376 | tf_op jit(solution)/shard_map/all_gather | solution.py:123
  66.8 136.1 %all-gather.10.cloned.1.call-start = ((), (), s32[]{:S(2)}) async-start(), calls=%async_computation.7 | async-start | bytes 1474560 | tf_op jit(solution)/shard_map/all_gather | solution.py:151
  133.1 13.0 %copy-start.5 = (bf16[1024,1,256]{0,2,1:T(8,128)(2,1)S(1)}, bf16[1024,1,256]{0,2,1:T(8,128)(2,1)}, u32[]{:S(2)}) copy-start(bf16[1024,1,256]{0,2,1:T(8,128)(2,1)} %all_gather.19) | copy-start | bytes 1572868
  133.1 13.0 %copy-start.7 = (pred[128,1024]{0,1:T(8,128)(4,1)S(1)}, pred[128,1024]{0,1:T(8,128)(4,1)}, u32[]{:S(2)}) copy-start(pred[128,1024]{0,1:T(8,128)(4,1)} %fusion.43) | copy-start | bytes 393220
  133.1 13.0 %copy-start.8 = (bf16[128,5,64]{2,0,1:T(8,128)(2,1)S(1)}, bf16[128,5,64]{2,0,1:T(8,128)(2,1)}, u32[]{:S(2)}) copy-start(bf16[128,5,64]{2,0,1:T(8,128)(2,1)} %get-tuple-element.16) | copy-start | bytes 245764
  133.1 13.0 %copy-start.9 = (bf16[128,5,64]{2,0,1:T(8,128)(2,1)S(1)}, bf16[128,5,64]{2,0,1:T(8,128)(2,1)}, u32[]{:S(2)}) copy-start(bf16[128,5,64]{2,0,1:T(8,128)(2,1)} %get-tuple-element.17) | copy-start | bytes 245764
  162.5 10.7 %copy-start.1 = (f32[1024,128,5]{1,0,2:T(8,128)S(1)}, f32[1024,128,5]{1,0,2:T(8,128)}, u32[]{:S(2)}) copy-start(f32[1024,128,5]{1,0,2:T(8,128)} %get-tuple-element.31) | copy-start | bytes 7864324
  173.2 1.0 copy-start.6
  173.2 1.1 copy-start.13
  175.8 67.4 %copy-start.2 = (bf16[1,128,640]{2,1,0:T(8,128)(2,1)S(1)}, bf16[1,128,640]{2,1,0:T(8,128)(2,1)}, u32[]{:S(2)}) copy-start(bf16[1,128,640]{2,1,0:T(8,128)(2,1)} %param.16) | copy-start | bytes 491524
  175.8 85.1 %copy-start.11 = (f32[640]{0:T(1024)S(1)}, f32[640]{0:T(1024)}, u32[]{:S(2)}) copy-start(f32[640]{0:T(1024)} %param.26) | copy-start | bytes 7684
  175.8 67.4 %reduce-scatter.7.cloned.1.call-start = ((), (), s32[]{:S(2)}) async-start(), calls=%async_computation.8 | async-start | bytes 1474560 | tf_op jit(solution)/shard_map/reduce_scatter | solution.py:155
  206.9 86.2 %all-gather.12.cloned.1.call-start = ((), (), s32[]{:S(2)}) async-start(), calls=%async_computation.9 | async-start | bytes 1474560 | tf_op jit(solution)/shard_map/all_gather | solution.py:165
  262.7 94.2 %reduce-scatter.9.cloned.1.call-start = ((), (), s32[]{:S(2)}) async-start(), calls=%async_computation.10 | async-start | bytes 8257536 | tf_op jit(solution)/shard_map/reduce_scatter | solution.py:169
  303.6 88.9 %all-gather.14.cloned.1.call-start = ((), (), s32[]{:S(2)}) async-start(), calls=%async_computation.11 | async-start | bytes 4128768 | tf_op jit(solution)/shard_map/all_gather | solution.py:174
  359.3 75.3 %copy-start.3 = (bf16[128,640]{1,0:T(8,128)(2,1)S(1)}, bf16[128,640]{1,0:T(8,128)(2,1)}, u32[]{:S(2)}) copy-start(bf16[128,640]{1,0:T(8,128)(2,1)} %reduce-scatter.7.cloned.1.call-done) | copy-start | bytes 491524
  359.3 75.3 %reduce-scatter.11.cloned.1.call-start = ((), (), s32[]{:S(2)}) async-start(), calls=%async_computation.12 | async-start | bytes 1474560 | tf_op jit(solution)/shard_map/reduce_scatter | solution.py:178
  399.3 414.8 %copy-start.10 = (f32[5120]{0:T(1024)S(1)}, f32[5120]{0:T(1024)}, u32[]{:S(2)}) copy-start(f32[5120]{0:T(1024)} %param.30) | copy-start | bytes 61444
  399.4 413.6 %all-reduce.2.cloned.1.call-start = ((), (), s32[]{:S(2)}) async-start(), calls=%async_computation.13 | async-start | bytes 655360 | tf_op jit(solution)/shard_map/psum | solution.py:196
  567.5 0.7 copy-start.4
Sparse Core Ops, SparseCore 0:
  26.1 35.0 all-gather.5
  66.4 41.5 reduce-scatter.4
  175.9 26.9 all-gather.9
  207.0 36.1 reduce-scatter.6
  262.8 30.2 all-gather.11
  303.7 53.1 reduce-scatter.8
  359.4 33.0 all-gather.13
  399.5 35.0 reduce-scatter.10
Sparse Core Ops, SparseCore 1:
  69.3 56.2 all-gather.7
  568.3 244.6 all-reduce.1
where the time goes:
time: 900 us; the launch traced here: 899 us
  waiting for transfers between devices  529 us (59%)
  blocking collectives  251 us (28%)
  matrix products  59.8 us (7%)
  other arithmetic  31.8 us (4%)
  between operations  15.8 us (2%)
  local copies, waits for them, and re-layouts  11.5 us (1%)
    psum x1, waiting for transfers between devices, on_device(): last_all = lax.psum(padded, ('grp', 'tok', 'mdl'))  243 us
    psum x1, blocking collectives, on_device(): req_total = lax.psum(req_squares, ('tok', 'mdl'))  128 us
    pmax x1, blocking collectives, on_device(): lax.pmax(jnp.max(logits, -1), ('grp', 'tok', 'mdl'))  74.3 us
    reduce_scatter x1, waiting for transfers between devices, on_device(): lax.psum_scatter(partial_ffn.astype(jnp.bfloat16), 'mdl', scatter_dimensi...  53.3 us
    reduce_scatter x1, waiting for transfers between devices, on_device(): lax.psum_scatter(partial_out.astype(jnp.bfloat16), 'tok', scatter_dimensi...  36.2 us
    all_gather x1, waiting for transfers between devices, on_device(): lax.all_gather(normed, 'tok', axis=0, tiled=True)  35.1 us
    reduce_scatter x1, waiting for transfers between devices, on_device(): lax.psum_scatter(partial_down.astype(jnp.bfloat16), 'tok', scatter_dimens...  35.1 us
    reduce_scatter x1, waiting for transfers between devices, on_device(): lax.psum_scatter(partial_qkv, 'mdl', scatter_dimension=0, tiled=True)  34.7 us
  transfers between devices with their start and end apart: 10, of which 9 were waited for; matrix products, arithmetic and copies ran while one was open for 2% of the time, Pallas kernels for 0%

commit v1 on v0

--- a/solution.py
+++ b/solution.py
@@ -193,7 +193,7 @@
         padded, last_part, (group_idx * req_count, mdl_idx * feat_dev)
     )
     req_total = lax.psum(req_squares, ("tok", "mdl"))
-    last_all = lax.psum(padded, ("grp", "tok", "mdl"))
+    last_all = jnp.sum(lax.all_gather(padded, ("grp", "tok", "mdl")), axis=0)
     req_norm = jnp.sqrt(req_total / (counts.astype(jnp.float32) * model_width) + EPS)
     last_normed = (
         last_all * lax.rsqrt(jnp.mean(last_all * last_all, -1, keepdims=True) + EPS) * final_gain

time: 900 us -> 796 us (0.88)
  waiting for transfers between devices: 529 us -> 400 us
  other arithmetic: 31.8 us -> 54.7 us
    psum x1 -> x0, waiting for transfers between devices: 243 us -> none  [on_device(): last_all = lax.psum(padded, ('grp', 'tok', 'mdl'))]
    all_gather x0 -> x1, waiting for transfers between devices: none -> 115 us  [on_device(): last_all = jnp.sum(lax.all_gather(padded, ('grp', 'tok', 'mdl')), axis=0)]
    reduce_sum x0 -> x1, other arithmetic: none -> 25.9 us  [on_device(): last_all = jnp.sum(lax.all_gather(padded, ('grp', 'tok', 'mdl')), axis=0)]
  transfers between devices with their start and end apart: 10 -> 10, of which waited for: 9 -> 9; matrix products, arithmetic and copies ran while one was open for 2% -> 3% of each run, Pallas kernels for 0% -> 0%
where the time goes in v1:
time: 796 us; the launch traced here: 795 us
  waiting for transfers between devices  400 us (50%)
  blocking collectives  252 us (32%)
  matrix products  59.7 us (8%)
  other arithmetic  54.7 us (7%)
  between operations  15.8 us (2%)
  local copies, waits for them, and re-layouts  12.2 us (2%)
    psum x1, blocking collectives, on_device(): req_total = lax.psum(req_squares, ('tok', 'mdl'))  130 us
    all_gather x1, waiting for transfers between devices, on_device(): last_all = jnp.sum(lax.all_gather(padded, ('grp', 'tok', 'mdl')), axis=0)  115 us
    pmax x1, blocking collectives, on_device(): lax.pmax(jnp.max(logits, -1), ('grp', 'tok', 'mdl'))  74.3 us
    reduce_scatter x1, waiting for transfers between devices, on_device(): lax.psum_scatter(partial_ffn.astype(jnp.bfloat16), 'mdl', scatter_dimensi...  53.3 us
    reduce_scatter x1, waiting for transfers between devices, on_device(): lax.psum_scatter(partial_out.astype(jnp.bfloat16), 'tok', scatter_dimensi...  36.2 us
    all_gather x1, waiting for transfers between devices, on_device(): lax.all_gather(normed, 'tok', axis=0, tiled=True)  35.1 us
    reduce_scatter x1, waiting for transfers between devices, on_device(): lax.psum_scatter(partial_down.astype(jnp.bfloat16), 'tok', scatter_dimens...  35.1 us
    reduce_scatter x1, waiting for transfers between devices, on_device(): lax.psum_scatter(partial_qkv, 'mdl', scatter_dimension=0, tiled=True)  34.7 us
  transfers between devices with their start and end apart: 10, of which 9 were waited for; matrix products, arithmetic and copies ran while one was open for 3% of the time, Pallas kernels for 0%

profile of v1, /device:TPU:1, one launch (start us, length us, event | category | flops | bytes accessed | tf_op | source)
XLA Modules:
  0.0 795.4 jit_solution(7946063939502936053)
XLA Ops:
  8.1 1.2 fusion.44
  9.2 15.0 %psum.21 = f32[128]{0:T(128)S(1)} all-reduce(f32[128]{0:T(128)S(1)} %fusion.44), channel_id=1, replica_groups=mesh['grp'=4,'tok'=8,'mdl'=8] {'mdl'}, use_global_device_ids=true, to_apply=%region_1.0 | all-reduce | flops 128 | bytes 1024 | tf_op jit(solution)/shard_map/psum | solution.py:62
  24.2 1.7 fusion.46
  26.0 35.1 %all-gather.7.cloned.1.call-done = bf16[1024,640]{1,0:T(8,128)(2,1)} async-done(((bf16[128,640]{1,0:T(8,128)(2,1)}), bf16[1024,640]{1,0:T(8,128)(2,1)}) %all-gather.7.cloned.1.call-update) | async-done | bytes 1310736 | tf_op jit(solution)/shard_map/all_gather | solution.py:68
  61.1 5.1 fusion.30
  66.3 0.5 all-gather.9.cloned.1.call-update
  66.9 0.7 constant_dynamic-slice_fusion.1
  67.6 0.1 convert_reduce_fusion
  67.8 0.2 reduce-window.7
  68.0 0.1 select_reduce_fusion.1
  68.2 0.7 fusion.60
  68.9 0.8 dynamic-slice_bitcast_fusion
  69.7 0.1 select_reduce_fusion.3
  69.8 1.0 multiply_cosine_fusion
  70.8 0.9 fusion.43
  71.6 1.6 broadcast_compare_fusion
  73.3 34.7 %reduce-scatter.5.cloned.1.call-done = f32[128,896]{0,1:T(8,128)} async-done(((f32[1024,896]{0,1:T(8,128)}), f32[128,896]{0,1:T(8,128)}) %reduce-scatter.5.cloned.1.call-update) | async-done | bytes 458768 | tf_op jit(solution)/shard_map/reduce_scatter | solution.py:72
  107.9 1.0 slice.59
  108.9 0.7 fusion.72
  109.7 1.1 copy.58
  110.8 1.8 copy.57
  112.6 0.8 slice_bitcast_fusion.10
  113.5 0.2 fusion.56
  113.7 0.8 fusion.59
  114.5 15.8 %all_gather.25 = bf16[1024,1,256]{0,2,1:T(8,128)(2,1)S(1)} all-gather(bf16[128,1,256]{0,2,1:T(8,128)(2,1)S(1)} %get-tuple-element.23), channel_id=1, replica_groups=mesh['grp'=4,'tok'=8,'mdl'=8] {'mdl'}, dimensions={0}, use_global_device_ids=true | all-gather | bytes 589824 | tf_op jit(solution)/shard_map/all_gather | solution.py:97
  130.4 1.3 subtract_convert_fusion
  131.7 0.6 copy-done.9
  132.4 3.1 fusion.10
  135.5 12.9 %fusion = (f32[128,5]{0,1:T(8,128)S(1)}, f32[128,5,8192]{2,0,1:T(8,128)}) fusion(pred[128,8192]{1,0:T(8,128)(4,1)} %broadcast_compare_fusion, bf16[8192,1,256]{2,0,1:T(8,128)(2,1)} %bitcast.152, bf16[128,5,64]{2,0,1:T(8,128)(2,1)} %copy-done.10, bf16[128,5,64]{2,0,1:T(8,128)(2,1)} %copy-done.9), kind=kOutput, calls=%fused_computation.2 | convolution fusion | flops 1358232960 | bytes 24447488 | tf_op jit(solution)/shard_map/rcgd,kcd->rcgk/dot_general | solution.py:129
  148.4 14.2 %fusion.21 = f32[1,128,128,5]{2,1,3,0:T(8,128)} fusion(bf16[8192,1,256]{2,0,1:T(8,128)(2,1)} %bitcast.153, f32[128,5,8192]{2,0,1:T(8,128)} %get-tuple-element.33, f32[128,5]{0,1:T(8,128)S(1)} %max.19, pred[128,8192]{1,0:T(8,128)(4,1)} %broadcast_compare_fusion), kind=kOutput, calls=%fused_computation.28 | convolution fusion | flops 1368391680 | bytes 24447488 | tf_op jit(solution)/shard_map/rcgk,kcd->rcgd/dot_general | solution.py:139
  162.6 10.9 %fusion.1 = f32[128,5]{0,1:T(8,128)S(1)} fusion(f32[128,5,8192]{2,0,1:T(8,128)} %get-tuple-element.33, f32[128,5]{0,1:T(8,128)S(1)} %max.19, pred[128,8192]{1,0:T(8,128)(4,1)} %broadcast_compare_fusion), kind=kLoop, calls=%fused_computation.3 | loop fusion | flops 26213760 | bytes 22025216 | tf_op jit(solution)/shard_map/reduce_sum | solution.py:138
  173.5 0.6 fusion.12
  174.2 0.3 copy-done.7
  174.5 0.1 copy-done.14
  174.6 1.5 fusion.39
  176.2 27.2 %all-gather.11.cloned.1.call-done = bf16[1024,640]{0,1:T(8,128)(2,1)} async-done(((bf16[128,640]{0,1:T(8,128)(2,1)}), bf16[1024,640]{0,1:T(8,128)(2,1)}) %all-gather.11.cloned.1.call-update) | async-done | bytes 1310736 | tf_op jit(solution)/shard_map/all_gather | solution.py:151
  203.4 4.0 convolution_convert_fusion.2
  207.4 36.2 %reduce-scatter.7.cloned.1.call-done = bf16[128,640]{1,0:T(8,128)(2,1)} async-done(((bf16[1024,640]{1,0:T(8,128)(2,1)}), bf16[128,640]{1,0:T(8,128)(2,1)}) %reduce-scatter.7.cloned.1.call-update) | async-done | bytes 163856 | tf_op jit(solution)/shard_map/reduce_scatter | solution.py:155
  243.7 1.1 multiply_reduce_fusion.2
  244.7 16.7 %psum.22 = f32[128]{0:T(128)S(1)} all-reduce(f32[128]{0:T(128)S(1)} %multiply_reduce_fusion.2), channel_id=1, replica_groups=mesh['grp'=4,'tok'=8,'mdl'=8] {'mdl'}, use_global_device_ids=true, to_apply=%region_14.15 | all-reduce | flops 128 | bytes 1024 | tf_op jit(solution)/shard_map/psum | solution.py:158
  261.4 1.7 multiply_convert_fusion.1
  263.2 30.4 %all-gather.13.cloned.1.call-done = bf16[1024,640]{1,0:T(8,128)(2,1)} async-done(((bf16[128,640]{1,0:T(8,128)(2,1)}), bf16[1024,640]{1,0:T(8,128)(2,1)}) %all-gather.13.cloned.1.call-update) | async-done | bytes 1310736 | tf_op jit(solution)/shard_map/all_gather | solution.py:165
  293.6 10.5 %convolution_convert_fusion = bf16[1024,3584]{1,0:T(8,128)(2,1)} fusion(bf16[1024,640]{1,0:T(8,128)(2,1)} %all-gather.13.cloned.1.call-done, bf16[640,1792]{1,0:T(8,128)(2,1)} %param.28, bf16[640,1792]{1,0:T(8,128)(2,1)} %param.27), kind=kOutput, calls=%fused_computation.8 | convolution fusion | flops 4710465536 | bytes 13238272 | tf_op jit(solution)/shard_map/dot_general | solution.py:164
  304.1 53.3 %reduce-scatter.9.cloned.1.call-done = bf16[128,3584]{1,0:T(8,128)(2,1)} async-done(((bf16[1024,3584]{1,0:T(8,128)(2,1)}), bf16[128,3584]{1,0:T(8,128)(2,1)}) %reduce-scatter.9.cloned.1.call-update) | async-done | bytes 917520 | tf_op jit(solution)/shard_map/reduce_scatter | solution.py:169
  357.4 1.4 convert_element_type.96
  358.7 1.0 fusion.42
  359.9 33.1 %all-gather.15.cloned.1.call-done = bf16[1024,1792]{1,0:T(8,128)(2,1)} async-done(((bf16[128,1792]{1,0:T(8,128)(2,1)}), bf16[1024,1792]{1,0:T(8,128)(2,1)}) %all-gather.15.cloned.1.call-update) | async-done | bytes 3670032 | tf_op jit(solution)/shard_map/all_gather | solution.py:174
  393.0 6.8 convolution_convert_fusion.1
  400.0 35.1 %reduce-scatter.11.cloned.1.call-done = bf16[128,640]{1,0:T(8,128)(2,1)} async-done(((bf16[1024,640]{1,0:T(8,128)(2,1)}), bf16[128,640]{1,0:T(8,128)(2,1)}) %reduce-scatter.11.cloned.1.call-update) | async-done | bytes 163856 | tf_op jit(solution)/shard_map/reduce_scatter | solution.py:178
  435.1 1.1 multiply_reduce_fusion.1
  436.2 0.7 copy-done.3
  436.9 0.2 select_reduce_fusion
  437.2 0.7 copy-done.5
  437.9 0.1 select_reduce_fusion.2
  438.0 0.7 copy.50
  438.8 130.4 %psum.23 = f32[4]{0:T(128)S(1)} all-reduce(f32[4]{0:T(128)S(1)} %select_reduce_fusion.2), channel_id=1, replica_groups=mesh['grp'=4,'tok'=8,'mdl'=8] {'tok','mdl'}, use_global_device_ids=true, to_apply=%region_19.20 | all-reduce | flops 4 | bytes 32 | tf_op jit(solution)/shard_map/psum | solution.py:195
  569.2 1.7 convert_bitcast_fusion
  570.8 114.5 %all-gather.17.cloned.1.call-done = f32[256,16,5120]{2,1,0:T(8,128)} async-done(((f32[1,16,5120]{2,1,0:T(8,128)}), f32[256,16,5120]{2,1,0:T(8,128)}) %all-gather.17.cloned.1.call-update) | async-done | bytes 83886096 | tf_op jit(solution)/shard_map/all_gather | solution.py:196
  685.4 25.9 %reduce_sum.128 = f32[16,5120]{1,0:T(8,128)S(1)} reduce(f32[256,16,5120]{2,1,0:T(8,128)} %all-gather.17.cloned.1.call-done, f32[]{:T(128)} %constant.87.clone.1), dimensions={0}, to_apply=%region_21.22 | reduce | flops 20889600 | bytes 84213760 | tf_op jit(solution)/shard_map/reduce_sum | solution.py:196
  711.2 0.2 multiply_reduce_fusion
  711.4 1.7 fusion.73
  713.1 0.1 reshape.447
  713.2 0.5 sqrt_bitcast_fusion
  713.7 74.3 %pmax.7 = f32[4,4]{1,0:T(4,128)} all-reduce(f32[4,4]{1,0:T(4,128)S(1)} %reshape.447), channel_id=1, replica_groups=mesh['grp'=4,'tok'=8,'mdl'=8] {'grp','tok','mdl'}, use_global_device_ids=true, to_apply=%region_24.25 | all-reduce | flops 16 | bytes 128 | tf_op jit(solution)/shard_map/pmax | solution.py:204
  (62 shorter events, 1.0 us)
Async XLA Ops:
  8.0 703.4 %copy-start = (bf16[300,5120]{1,0:T(8,128)(2,1)S(1)}, bf16[300,5120]{1,0:T(8,128)(2,1)}, u32[]{:S(2)}) copy-start(bf16[300,5120]{1,0:T(8,128)(2,1)} %param.31) | copy-start | bytes 9216004
  8.0 53.1 %all-gather.7.cloned.1.call-start = ((), (), s32[]{:S(2)}) async-start(), calls=%async_computation.4 | async-start | bytes 1474560 | tf_op jit(solution)/shard_map/all_gather | solution.py:68
  25.9 82.0 %reduce-scatter.5.cloned.1.call-start = ((), (), s32[]{:S(2)}) async-start(), calls=%async_computation.5 | async-start | bytes 4128768 | tf_op jit(solution)/shard_map/reduce_scatter | solution.py:72
  66.2 1.7 copy-start.13
  66.3 69.2 %all-gather.9.cloned.1.call-start = ((), (), s32[]{:S(2)}) async-start(), calls=%async_computation.6 | async-start | bytes 4325376 | tf_op jit(solution)/shard_map/all_gather | solution.py:123
  66.8 136.5 %all-gather.11.cloned.1.call-start = ((), (), s32[]{:S(2)}) async-start(), calls=%async_computation.7 | async-start | bytes 1474560 | tf_op jit(solution)/shard_map/all_gather | solution.py:151
  130.4 1.3 copy-start.6
  131.6 0.7 copy-start.9
  131.7 0.7 copy-start.10
  162.6 10.9 %copy-start.1 = (f32[1024,128,5]{1,0,2:T(8,128)S(1)}, f32[1024,128,5]{1,0,2:T(8,128)}, u32[]{:S(2)}) copy-start(f32[1024,128,5]{1,0,2:T(8,128)} %get-tuple-element.31) | copy-start | bytes 7864324
  162.6 11.0 %copy-start.8 = (pred[128,1024]{0,1:T(8,128)(4,1)S(1)}, pred[128,1024]{0,1:T(8,128)(4,1)}, u32[]{:S(2)}) copy-start(pred[128,1024]{0,1:T(8,128)(4,1)} %fusion.43) | copy-start | bytes 393220
  173.5 1.0 copy-start.7
  173.5 1.1 copy-start.14
  176.1 67.6 %copy-start.2 = (bf16[1,128,640]{2,1,0:T(8,128)(2,1)S(1)}, bf16[1,128,640]{2,1,0:T(8,128)(2,1)}, u32[]{:S(2)}) copy-start(bf16[1,128,640]{2,1,0:T(8,128)(2,1)} %param.16) | copy-start | bytes 491524
  176.1 85.3 %copy-start.12 = (f32[640]{0:T(1024)S(1)}, f32[640]{0:T(1024)}, u32[]{:S(2)}) copy-start(f32[640]{0:T(1024)} %param.26) | copy-start | bytes 7684
  176.1 67.5 %reduce-scatter.7.cloned.1.call-start = ((), (), s32[]{:S(2)}) async-start(), calls=%async_computation.8 | async-start | bytes 1474560 | tf_op jit(solution)/shard_map/reduce_scatter | solution.py:155
  207.4 86.2 %all-gather.13.cloned.1.call-start = ((), (), s32[]{:S(2)}) async-start(), calls=%async_computation.9 | async-start | bytes 1474560 | tf_op jit(solution)/shard_map/all_gather | solution.py:165
  263.1 94.2 %reduce-scatter.9.cloned.1.call-start = ((), (), s32[]{:S(2)}) async-start(), calls=%async_computation.10 | async-start | bytes 8257536 | tf_op jit(solution)/shard_map/reduce_scatter | solution.py:169
  304.1 88.9 %all-gather.15.cloned.1.call-start = ((), (), s32[]{:S(2)}) async-start(), calls=%async_computation.11 | async-start | bytes 4128768 | tf_op jit(solution)/shard_map/all_gather | solution.py:174
  359.8 75.3 %copy-start.4 = (bf16[128,640]{1,0:T(8,128)(2,1)S(1)}, bf16[128,640]{1,0:T(8,128)(2,1)}, u32[]{:S(2)}) copy-start(bf16[128,640]{1,0:T(8,128)(2,1)} %reduce-scatter.7.cloned.1.call-done) | copy-start | bytes 491524
  359.8 75.3 %reduce-scatter.11.cloned.1.call-start = ((), (), s32[]{:S(2)}) async-start(), calls=%async_computation.12 | async-start | bytes 1474560 | tf_op jit(solution)/shard_map/reduce_scatter | solution.py:178
  399.9 285.5 %all-gather.17.cloned.1.call-start = ((), (), s32[]{:S(2)}) async-start(), calls=%async_computation.13 | async-start | bytes 84213760 | tf_op jit(solution)/shard_map/all_gather | solution.py:196
  436.2 0.7 copy-start.3
  437.1 0.7 copy-start.5
  570.8 140.6 %copy-start.11 = (f32[5120]{0:T(1024)S(1)}, f32[5120]{0:T(1024)}, u32[]{:S(2)}) copy-start(f32[5120]{0:T(1024)} %param.30) | copy-start | bytes 61444
Sparse Core Ops, SparseCore 0:
  26.1 35.0 all-gather.6
  66.4 41.5 reduce-scatter.4
  176.2 27.1 all-gather.10
  207.5 36.1 reduce-scatter.6
  263.3 30.2 all-gather.12
  304.2 53.1 reduce-scatter.8
  359.9 33.0 all-gather.14
  400.0 35.0 reduce-scatter.10
Sparse Core Ops, SparseCore 1:
  69.3 56.2 all-gather.8
  438.0 247.3 all-gather.16
